TPU v7x, 512 devices: a whole 4x4x16 slice. The times are simulated.
512 devices in a mesh: cand: 8 (over y, core), doc: 64 (over z, x).
Axes of the slice: x: 4, y: 4, z: 16, core: 2. Of those that a mesh axis runs over, the one named last changes fastest.
Arguments:
- queries: bfloat16 [8192, 8192], P('doc'), may hold values from -6 to 50
- keys_values: bfloat16 [2, 8192, 1024], P(None, 'doc', 'cand'), may hold values from -6 to 50
- factors: float32 [8, 64], P('cand'), may hold values from 1 to 16
- lengths: int32 [16], replicated, may hold values from 1 to 1024, 8192 in all
Outputs:
- attended: bfloat16 [8, 8192, 8192], P('cand', 'doc')
All inputs are finite; a program needn't handle non-finite values.
Results may differ from a plain program's by a relative error of at most 0.0053.
Values may be sent and summed in bfloat16 or wider, within the bound.
No kernel may reach another device: no remote copies, remote signals or barrier semaphores. Data moves between devices by JAX's collectives and lax.ppermute only.
A program may use at most 64 MiB of HBM per device.

v0:
```python
import math
import jax
import jax.numpy as jnp
from jax import lax
from jax.sharding import PartitionSpec as P

H = 64
KVH = 8
HD = 128
SPAN = 8
ROPE_BASE = 500000.0


def passed_along(value, axis, steps):
    count = lax.axis_size(axis)
    first, last = (max(0, -steps), min(count, count - steps))
    return lax.ppermute(value, axis, [(source, source + steps) for source in range(first, last)])


def locate(index_rows, lengths):
    ends = jnp.cumsum(lengths)
    starts = ends - lengths
    docid = jnp.sum((index_rows[:, None] >= ends[None, :]).astype(jnp.int32), axis=1)
    onehot = docid[:, None] == jnp.arange(lengths.shape[0], dtype=jnp.int32)[None, :]
    first_row = jnp.sum(jnp.where(onehot, starts[None, :], 0), axis=1)
    valid = index_rows >= 0
    return (jnp.where(valid, docid, -1), jnp.where(valid, index_rows - first_row, 0))


def rotate(values, offsets, factor):
    row_count = values.shape[0]
    heads_here = values.shape[1] // HD
    half_dim = HD // 2
    shaped = values.reshape(row_count, heads_here, HD).astype(jnp.float32)
    inverse = jnp.power(ROPE_BASE, -2.0 * jnp.arange(half_dim, dtype=jnp.float32) / HD) / factor
    angles = offsets.astype(jnp.float32)[:, None] * inverse[None, :]
    cosine = jnp.cos(angles)[:, None, :]
    sine = jnp.sin(angles)[:, None, :]
    first_half = shaped[..., :half_dim]
    second_half = shaped[..., half_dim:]
    turned = jnp.concatenate(
        [first_half * cosine - second_half * sine, second_half * cosine + first_half * sine],
        axis=-1,
    )
    return turned.reshape(row_count, heads_here * HD).astype(jnp.bfloat16)


def attend_group(query_rot, key_rot, value_rows, allowed):
    row_count = query_rot.shape[0]
    group_size = H // KVH
    q_part = query_rot.reshape(row_count, group_size, HD)
    scale = 1.0 / math.sqrt(HD)
    scores = jnp.einsum("rgd,wd->rgw", q_part, key_rot, preferred_element_type=jnp.float32) * scale
    scores = jnp.where(allowed[:, None, :], scores, -1e30)
    largest = jnp.max(scores, axis=-1, keepdims=True)
    expw = jnp.exp(scores - largest)
    total = jnp.sum(expw, axis=-1, keepdims=True)
    weights = expw.astype(jnp.bfloat16)
    numer = jnp.einsum("rgw,wd->rgd", weights, value_rows, preferred_element_type=jnp.float32)
    return (numer / total).astype(jnp.bfloat16).reshape(row_count, group_size * HD)


def on_device(queries, keys_values, factors, lengths):
    row_count = queries.shape[0]
    group_width = queries.shape[1] // KVH
    device = lax.axis_index("doc")
    group = lax.axis_index("cand")
    query_index = device * row_count + jnp.arange(row_count, dtype=jnp.int32)
    key_index = (device - SPAN) * row_count + jnp.arange((SPAN + 1) * row_count, dtype=jnp.int32)
    every_factor = lax.all_gather(factors, "cand", axis=0, tiled=True)
    pieces = []
    for distance in range(SPAN, 0, -1):
        pieces.append(passed_along(keys_values, "doc", distance))
    pieces.append(keys_values)
    window = jnp.concatenate(pieces, axis=1)
    query_doc, query_offset = locate(query_index, lengths)
    key_doc, key_offset = locate(key_index, lengths)
    allowed = (
        (key_doc[None, :] == query_doc[:, None])
        & (key_index[None, :] <= query_index[:, None])
        & (key_doc[None, :] >= 0)
    )
    own_queries = lax.dynamic_slice_in_dim(queries, group * group_width, group_width, 1)

    def per_candidate(factor):
        query_rot = rotate(own_queries, query_offset, factor)
        key_rot = rotate(window[0], key_offset, factor)
        return attend_group(query_rot, key_rot, window[1], allowed)

    mixed = lax.map(per_candidate, every_factor)
    return lax.all_to_all(mixed, "cand", 0, 2, tiled=True)


def solution(mesh):
    placed = (P("doc", None), P(None, "doc", "cand"), P("cand", None), P())
    return jax.shard_map(
        on_device, mesh=mesh, in_specs=placed, out_specs=P("cand", "doc", None), check_vma=False
    )
```

profile of v0, /device:TPU:32, one launch (start us, length us, event | category | flops | bytes accessed | tf_op | source)
XLA Modules:
  0.0 206.3 jit_solution(13450548175812455790)
XLA Ops:
  1.1 5.2 %collective-permute-start = (bf16[2,128,128]{1,2,0:T(8,128)(2,1)S(1)}, bf16[2,128,128]{1,2,0:T(8,128)(2,1)S(1)}, u32[]{:S(2)}, u32[]{:S(2)}) collective-permute-start(bf16[2,128,128]{1,2,0:T(8,128)(2,1)S(1)} %copy.37), channel_id=1, source_target_pairs={{0,8},{1,9},{2,10},{3,11},{4,12},{5,13},{6,14},{7,15},{8,16},{9,17... | collective-permute-start | bytes 196616 | tf_op jit(solution)/shard_map/ppermute | solution.py:17
  6.3 7.2 %collective-permute-start.1 = (bf16[2,128,128]{1,2,0:T(8,128)(2,1)S(1)}, bf16[2,128,128]{1,2,0:T(8,128)(2,1)S(1)}, u32[]{:S(2)}, u32[]{:S(2)}) collective-permute-start(bf16[2,128,128]{1,2,0:T(8,128)(2,1)S(1)} %copy.37), channel_id=1, source_target_pairs={{0,7},{1,8},{2,9},{3,10},{4,11},{5,12},{6,13},{7,14},{8,15},{9,16}... | collective-permute-start | bytes 196616 | tf_op jit(solution)/shard_map/ppermute | solution.py:17
  13.5 5.4 %collective-permute-start.2 = (bf16[2,128,128]{1,2,0:T(8,128)(2,1)S(1)}, bf16[2,128,128]{1,2,0:T(8,128)(2,1)S(1)}, u32[]{:S(2)}, u32[]{:S(2)}) collective-permute-start(bf16[2,128,128]{1,2,0:T(8,128)(2,1)S(1)} %copy.37), channel_id=1, source_target_pairs={{0,6},{1,7},{2,8},{3,9},{4,10},{5,11},{6,12},{7,13},{8,14},{9,15},... | collective-permute-start | bytes 196616 | tf_op jit(solution)/shard_map/ppermute | solution.py:17
  19.0 4.1 %collective-permute-start.3 = (bf16[2,128,128]{1,2,0:T(8,128)(2,1)S(1)}, bf16[2,128,128]{1,2,0:T(8,128)(2,1)S(1)}, u32[]{:S(2)}, u32[]{:S(2)}) collective-permute-start(bf16[2,128,128]{1,2,0:T(8,128)(2,1)S(1)} %copy.37), channel_id=1, source_target_pairs={{0,5},{1,6},{2,7},{3,8},{4,9},{5,10},{6,11},{7,12},{8,13},{9,14},{... | collective-permute-start | bytes 196616 | tf_op jit(solution)/shard_map/ppermute | solution.py:17
  23.1 5.0 %collective-permute-start.4 = (bf16[2,128,128]{1,2,0:T(8,128)(2,1)S(1)}, bf16[2,128,128]{1,2,0:T(8,128)(2,1)S(1)}, u32[]{:S(2)}, u32[]{:S(2)}) collective-permute-start(bf16[2,128,128]{1,2,0:T(8,128)(2,1)S(1)} %copy.37), channel_id=1, source_target_pairs={{0,4},{1,5},{2,6},{3,7},{4,8},{5,9},{6,10},{7,11},{8,12},{9,13},{1... | collective-permute-start | bytes 196616 | tf_op jit(solution)/shard_map/ppermute | solution.py:17
  32.0 11.5 %all-gather = f32[8,1,64]{2,1,0:T(1,128)} all-gather(f32[1,1,64]{2,1,0:T(1,128)} %bitcast.51), channel_id=1, replica_groups=mesh['cand'=8,'doc'=64] {'cand'}, dimensions={0}, use_global_device_ids=true | all-gather | bytes 2304 | tf_op jit(solution)/shard_map/all_gather | solution.py:70
  43.6 4.7 %collective-permute-start.5 = (bf16[2,128,128]{1,2,0:T(8,128)(2,1)S(1)}, bf16[2,128,128]{1,2,0:T(8,128)(2,1)S(1)}, u32[]{:S(2)}, u32[]{:S(2)}) collective-permute-start(bf16[2,128,128]{1,2,0:T(8,128)(2,1)S(1)} %copy.37), channel_id=1, source_target_pairs={{0,3},{1,4},{2,5},{3,6},{4,7},{5,8},{6,9},{7,10},{8,11},{9,12},{10... | collective-permute-start | bytes 196616 | tf_op jit(solution)/shard_map/ppermute | solution.py:17
  48.3 3.4 %collective-permute-start.6 = (bf16[2,128,128]{1,2,0:T(8,128)(2,1)S(1)}, bf16[2,128,128]{1,2,0:T(8,128)(2,1)S(1)}, u32[]{:S(2)}, u32[]{:S(2)}) collective-permute-start(bf16[2,128,128]{1,2,0:T(8,128)(2,1)S(1)} %copy.37), channel_id=1, source_target_pairs={{0,2},{1,3},{2,4},{3,5},{4,6},{5,7},{6,8},{7,9},{8,10},{9,11},{10,... | collective-permute-start | bytes 196616 | tf_op jit(solution)/shard_map/ppermute | solution.py:17
  53.9 3.0 %collective-permute-done.6 = bf16[2,128,128]{1,2,0:T(8,128)(2,1)S(1)} collective-permute-done((bf16[2,128,128]{1,2,0:T(8,128)(2,1)S(1)}, bf16[2,128,128]{1,2,0:T(8,128)(2,1)S(1)}, u32[]{:S(2)}, u32[]{:S(2)}) %collective-permute-start.6) | collective-permute-done | bytes 65568 | tf_op jit(solution)/shard_map/ppermute | solution.py:17
  56.9 3.1 %collective-permute-done.7 = bf16[2,128,128]{1,2,0:T(8,128)(2,1)S(1)} collective-permute-done((bf16[2,128,128]{1,2,0:T(8,128)(2,1)S(1)}, bf16[2,128,128]{1,2,0:T(8,128)(2,1)S(1)}, u32[]{:S(2)}, u32[]{:S(2)}) %collective-permute-start.7) | collective-permute-done | bytes 65568 | tf_op jit(solution)/shard_map/ppermute | solution.py:17
  60.9 109.5 %while.13 = (s32[]{:T(128)}, bf16[8,128,1024]{1,2,0:T(8,128)(2,1)}, bf16[128,1024]{0,1:T(8,128)(2,1)S(1)}, f32[128,1]{0,1:T(1,128)S(1)}, f32[8,64]{1,0:T(8,128)}...) while((s32[]{:T(128)}, bf16[8,128,1024]{1,2,0:T(8,128)(2,1)}, ...), condition=%wide.region_8.9_spmd.clone, body=%wide.region_5.8_spmd.clone.sunk | while | flops 615544960 | bytes 23285628 | solution.py:90
  66.7 1.9 fusion.47
  69.5 2.3 %fusion.49 = (f32[128,8]{0,1:T(8,128)S(1)}, f32[128,8,1152]{2,0,1:T(8,128)S(1)}) fusion(bf16[1152,1,64]{0,2,1:T(8,128)(2,1)S(1)} %get-tuple-element.261, bf16[1152,1,64]{0,2,1:T(8,128)(2,1)S(1)} %get-tuple-element.262, bf16[128,8,64]{2,0,1:T(8,128)(2,1)} %get-tuple-element.267, bf16[128,8,64]{2,0,1:T(8,128)(2,1)} %get-tuple-element.268, ...), kind=kOutput, calls=%fused_computation.66.clone.1 | convolution fusion | flops 306641920 | bytes 5427200 | tf_op jit(solution)/shard_map/while/body/eval_jaxpr/rgd,wd->rgw/dot_general | solution.py:53
  83.2 2.3 %fusion.49 = (f32[128,8]{0,1:T(8,128)S(1)}, f32[128,8,1152]{2,0,1:T(8,128)S(1)}) fusion(bf16[1152,1,64]{0,2,1:T(8,128)(2,1)S(1)} %get-tuple-element.261, bf16[1152,1,64]{0,2,1:T(8,128)(2,1)S(1)} %get-tuple-element.262, bf16[128,8,64]{2,0,1:T(8,128)(2,1)} %get-tuple-element.267, bf16[128,8,64]{2,0,1:T(8,128)(2,1)} %get-tuple-element.268, ...), kind=kOutput, calls=%fused_computation.66.clone.1 | convolution fusion | flops 306641920 | bytes 5427200 | tf_op jit(solution)/shard_map/while/body/eval_jaxpr/rgd,wd->rgw/dot_general | solution.py:53
  94.1 1.9 fusion.47
  96.9 2.3 %fusion.49 = (f32[128,8]{0,1:T(8,128)S(1)}, f32[128,8,1152]{2,0,1:T(8,128)S(1)}) fusion(bf16[1152,1,64]{0,2,1:T(8,128)(2,1)S(1)} %get-tuple-element.261, bf16[1152,1,64]{0,2,1:T(8,128)(2,1)S(1)} %get-tuple-element.262, bf16[128,8,64]{2,0,1:T(8,128)(2,1)} %get-tuple-element.267, bf16[128,8,64]{2,0,1:T(8,128)(2,1)} %get-tuple-element.268, ...), kind=kOutput, calls=%fused_computation.66.clone.1 | convolution fusion | flops 306641920 | bytes 5427200 | tf_op jit(solution)/shard_map/while/body/eval_jaxpr/rgd,wd->rgw/dot_general | solution.py:53
  110.6 2.3 %fusion.49 = (f32[128,8]{0,1:T(8,128)S(1)}, f32[128,8,1152]{2,0,1:T(8,128)S(1)}) fusion(bf16[1152,1,64]{0,2,1:T(8,128)(2,1)S(1)} %get-tuple-element.261, bf16[1152,1,64]{0,2,1:T(8,128)(2,1)S(1)} %get-tuple-element.262, bf16[128,8,64]{2,0,1:T(8,128)(2,1)} %get-tuple-element.267, bf16[128,8,64]{2,0,1:T(8,128)(2,1)} %get-tuple-element.268, ...), kind=kOutput, calls=%fused_computation.66.clone.1 | convolution fusion | flops 306641920 | bytes 5427200 | tf_op jit(solution)/shard_map/while/body/eval_jaxpr/rgd,wd->rgw/dot_general | solution.py:53
  121.4 1.9 fusion.47
  124.3 2.3 %fusion.49 = (f32[128,8]{0,1:T(8,128)S(1)}, f32[128,8,1152]{2,0,1:T(8,128)S(1)}) fusion(bf16[1152,1,64]{0,2,1:T(8,128)(2,1)S(1)} %get-tuple-element.261, bf16[1152,1,64]{0,2,1:T(8,128)(2,1)S(1)} %get-tuple-element.262, bf16[128,8,64]{2,0,1:T(8,128)(2,1)} %get-tuple-element.267, bf16[128,8,64]{2,0,1:T(8,128)(2,1)} %get-tuple-element.268, ...), kind=kOutput, calls=%fused_computation.66.clone.1 | convolution fusion | flops 306641920 | bytes 5427200 | tf_op jit(solution)/shard_map/while/body/eval_jaxpr/rgd,wd->rgw/dot_general | solution.py:53
  138.0 2.3 %fusion.49 = (f32[128,8]{0,1:T(8,128)S(1)}, f32[128,8,1152]{2,0,1:T(8,128)S(1)}) fusion(bf16[1152,1,64]{0,2,1:T(8,128)(2,1)S(1)} %get-tuple-element.261, bf16[1152,1,64]{0,2,1:T(8,128)(2,1)S(1)} %get-tuple-element.262, bf16[128,8,64]{2,0,1:T(8,128)(2,1)} %get-tuple-element.267, bf16[128,8,64]{2,0,1:T(8,128)(2,1)} %get-tuple-element.268, ...), kind=kOutput, calls=%fused_computation.66.clone.1 | convolution fusion | flops 306641920 | bytes 5427200 | tf_op jit(solution)/shard_map/while/body/eval_jaxpr/rgd,wd->rgw/dot_general | solution.py:53
  151.6 2.3 %fusion.49 = (f32[128,8]{0,1:T(8,128)S(1)}, f32[128,8,1152]{2,0,1:T(8,128)S(1)}) fusion(bf16[1152,1,64]{0,2,1:T(8,128)(2,1)S(1)} %get-tuple-element.261, bf16[1152,1,64]{0,2,1:T(8,128)(2,1)S(1)} %get-tuple-element.262, bf16[128,8,64]{2,0,1:T(8,128)(2,1)} %get-tuple-element.267, bf16[128,8,64]{2,0,1:T(8,128)(2,1)} %get-tuple-element.268, ...), kind=kOutput, calls=%fused_computation.66.clone.1 | convolution fusion | flops 306641920 | bytes 5427200 | tf_op jit(solution)/shard_map/while/body/eval_jaxpr/rgd,wd->rgw/dot_general | solution.py:53
  165.3 2.3 %fusion.49 = (f32[128,8]{0,1:T(8,128)S(1)}, f32[128,8,1152]{2,0,1:T(8,128)S(1)}) fusion(bf16[1152,1,64]{0,2,1:T(8,128)(2,1)S(1)} %get-tuple-element.261, bf16[1152,1,64]{0,2,1:T(8,128)(2,1)S(1)} %get-tuple-element.262, bf16[128,8,64]{2,0,1:T(8,128)(2,1)} %get-tuple-element.267, bf16[128,8,64]{2,0,1:T(8,128)(2,1)} %get-tuple-element.268, ...), kind=kOutput, calls=%fused_computation.66.clone.1 | convolution fusion | flops 306641920 | bytes 5427200 | tf_op jit(solution)/shard_map/while/body/eval_jaxpr/rgd,wd->rgw/dot_general | solution.py:53
  170.4 31.8 %all_to_all.18 = bf16[8,128,1024]{1,2,0:T(8,128)(2,1)} all-to-all(bf16[8,128,1024]{1,2,0:T(8,128)(2,1)} %get-tuple-element.110), channel_id=1, replica_groups=mesh['cand'=8,'doc'=64] {'cand'}, dimensions={0} | all-to-all | bytes 4194304 | tf_op jit(solution)/shard_map/all_to_all | solution.py:91
  202.2 4.1 %copy.48 = bf16[1,128,8192]{2,1,0:T(8,128)(2,1)} copy(bf16[1,128,8192]{1,2,0:T(8,128)(2,1)} %bitcast.47) | data formatting | bytes 4194304 | tf_op jit(solution)/shard_map/all_to_all | solution.py:91
  (205 shorter events, 92.7 us)
Async XLA Ops:
  0.0 31.8 %copy-start = (bf16[128,8192]{1,0:T(8,128)(2,1)S(1)}, bf16[128,8192]{1,0:T(8,128)(2,1)}, u32[]{:S(2)}) copy-start(bf16[128,8192]{1,0:T(8,128)(2,1)} %param.6) | copy-start | bytes 6291460
  1.1 42.5 %collective-permute-start = (bf16[2,128,128]{1,2,0:T(8,128)(2,1)S(1)}, bf16[2,128,128]{1,2,0:T(8,128)(2,1)S(1)}, u32[]{:S(2)}, u32[]{:S(2)}) collective-permute-start(bf16[2,128,128]{1,2,0:T(8,128)(2,1)S(1)} %copy.37), channel_id=1, source_target_pairs={{0,8},{1,9},{2,10},{3,11},{4,12},{5,13},{6,14},{7,15},{8,16},{9,17... | collective-permute-start | bytes 196616 | tf_op jit(solution)/shard_map/ppermute | solution.py:17
  6.3 42.0 %collective-permute-start.1 = (bf16[2,128,128]{1,2,0:T(8,128)(2,1)S(1)}, bf16[2,128,128]{1,2,0:T(8,128)(2,1)S(1)}, u32[]{:S(2)}, u32[]{:S(2)}) collective-permute-start(bf16[2,128,128]{1,2,0:T(8,128)(2,1)S(1)} %copy.37), channel_id=1, source_target_pairs={{0,7},{1,8},{2,9},{3,10},{4,11},{5,12},{6,13},{7,14},{8,15},{9,16}... | collective-permute-start | bytes 196616 | tf_op jit(solution)/shard_map/ppermute | solution.py:17
  13.5 38.3 %collective-permute-start.2 = (bf16[2,128,128]{1,2,0:T(8,128)(2,1)S(1)}, bf16[2,128,128]{1,2,0:T(8,128)(2,1)S(1)}, u32[]{:S(2)}, u32[]{:S(2)}) collective-permute-start(bf16[2,128,128]{1,2,0:T(8,128)(2,1)S(1)} %copy.37), channel_id=1, source_target_pairs={{0,6},{1,7},{2,8},{3,9},{4,10},{5,11},{6,12},{7,13},{8,14},{9,15},... | collective-permute-start | bytes 196616 | tf_op jit(solution)/shard_map/ppermute | solution.py:17
  19.0 34.8 %collective-permute-start.3 = (bf16[2,128,128]{1,2,0:T(8,128)(2,1)S(1)}, bf16[2,128,128]{1,2,0:T(8,128)(2,1)S(1)}, u32[]{:S(2)}, u32[]{:S(2)}) collective-permute-start(bf16[2,128,128]{1,2,0:T(8,128)(2,1)S(1)} %copy.37), channel_id=1, source_target_pairs={{0,5},{1,6},{2,7},{3,8},{4,9},{5,10},{6,11},{7,12},{8,13},{9,14},{... | collective-permute-start | bytes 196616 | tf_op jit(solution)/shard_map/ppermute | solution.py:17
  23.1 30.7 %collective-permute-start.4 = (bf16[2,128,128]{1,2,0:T(8,128)(2,1)S(1)}, bf16[2,128,128]{1,2,0:T(8,128)(2,1)S(1)}, u32[]{:S(2)}, u32[]{:S(2)}) collective-permute-start(bf16[2,128,128]{1,2,0:T(8,128)(2,1)S(1)} %copy.37), channel_id=1, source_target_pairs={{0,4},{1,5},{2,6},{3,7},{4,8},{5,9},{6,10},{7,11},{8,12},{9,13},{1... | collective-permute-start | bytes 196616 | tf_op jit(solution)/shard_map/ppermute | solution.py:17
  43.6 10.2 %collective-permute-start.5 = (bf16[2,128,128]{1,2,0:T(8,128)(2,1)S(1)}, bf16[2,128,128]{1,2,0:T(8,128)(2,1)S(1)}, u32[]{:S(2)}, u32[]{:S(2)}) collective-permute-start(bf16[2,128,128]{1,2,0:T(8,128)(2,1)S(1)} %copy.37), channel_id=1, source_target_pairs={{0,3},{1,4},{2,5},{3,6},{4,7},{5,8},{6,9},{7,10},{8,11},{9,12},{10... | collective-permute-start | bytes 196616 | tf_op jit(solution)/shard_map/ppermute | solution.py:17
  48.3 8.6 %collective-permute-start.6 = (bf16[2,128,128]{1,2,0:T(8,128)(2,1)S(1)}, bf16[2,128,128]{1,2,0:T(8,128)(2,1)S(1)}, u32[]{:S(2)}, u32[]{:S(2)}) collective-permute-start(bf16[2,128,128]{1,2,0:T(8,128)(2,1)S(1)} %copy.37), channel_id=1, source_target_pairs={{0,2},{1,3},{2,4},{3,5},{4,6},{5,7},{6,8},{7,9},{8,10},{9,11},{10,... | collective-permute-start | bytes 196616 | tf_op jit(solution)/shard_map/ppermute | solution.py:17
  51.8 8.3 %collective-permute-start.7 = (bf16[2,128,128]{1,2,0:T(8,128)(2,1)S(1)}, bf16[2,128,128]{1,2,0:T(8,128)(2,1)S(1)}, u32[]{:S(2)}, u32[]{:S(2)}) collective-permute-start(bf16[2,128,128]{1,2,0:T(8,128)(2,1)S(1)} %copy.37), channel_id=1, source_target_pairs={{0,1},{1,2},{2,3},{3,4},{4,5},{5,6},{6,7},{7,8},{8,9},{9,10},{10,1... | collective-permute-start | bytes 196616 | tf_op jit(solution)/shard_map/ppermute | solution.py:17
  69.5 3.3 %copy-start.2 = (bf16[2,1152,128]{1,2,0:T(8,128)(2,1)S(1)}, bf16[2,1152,128]{1,2,0:T(8,128)(2,1)}, u32[]{:S(2)}) copy-start(bf16[2,1152,128]{1,2,0:T(8,128)(2,1)} %get-tuple-element.304) | copy-start | bytes 1769476 | tf_op jit(solution)/shard_map/while
  71.8 2.8 %copy-start.6 = (f32[128,1]{0,1:T(1,128)S(1)}, f32[128,1]{0,1:T(1,128)}, u32[]{:S(2)}) copy-start(f32[128,1]{0,1:T(1,128)} %copy-done.5) | copy-start | bytes 1540 | tf_op jit(solution)/shard_map/while
  83.2 3.3 %copy-start.2 = (bf16[2,1152,128]{1,2,0:T(8,128)(2,1)S(1)}, bf16[2,1152,128]{1,2,0:T(8,128)(2,1)}, u32[]{:S(2)}) copy-start(bf16[2,1152,128]{1,2,0:T(8,128)(2,1)} %get-tuple-element.304) | copy-start | bytes 1769476 | tf_op jit(solution)/shard_map/while
  85.5 2.8 %copy-start.6 = (f32[128,1]{0,1:T(1,128)S(1)}, f32[128,1]{0,1:T(1,128)}, u32[]{:S(2)}) copy-start(f32[128,1]{0,1:T(1,128)} %copy-done.5) | copy-start | bytes 1540 | tf_op jit(solution)/shard_map/while
  96.9 3.3 %copy-start.2 = (bf16[2,1152,128]{1,2,0:T(8,128)(2,1)S(1)}, bf16[2,1152,128]{1,2,0:T(8,128)(2,1)}, u32[]{:S(2)}) copy-start(bf16[2,1152,128]{1,2,0:T(8,128)(2,1)} %get-tuple-element.304) | copy-start | bytes 1769476 | tf_op jit(solution)/shard_map/while
  99.2 2.8 %copy-start.6 = (f32[128,1]{0,1:T(1,128)S(1)}, f32[128,1]{0,1:T(1,128)}, u32[]{:S(2)}) copy-start(f32[128,1]{0,1:T(1,128)} %copy-done.5) | copy-start | bytes 1540 | tf_op jit(solution)/shard_map/while
  110.6 3.3 %copy-start.2 = (bf16[2,1152,128]{1,2,0:T(8,128)(2,1)S(1)}, bf16[2,1152,128]{1,2,0:T(8,128)(2,1)}, u32[]{:S(2)}) copy-start(bf16[2,1152,128]{1,2,0:T(8,128)(2,1)} %get-tuple-element.304) | copy-start | bytes 1769476 | tf_op jit(solution)/shard_map/while
  112.9 2.8 %copy-start.6 = (f32[128,1]{0,1:T(1,128)S(1)}, f32[128,1]{0,1:T(1,128)}, u32[]{:S(2)}) copy-start(f32[128,1]{0,1:T(1,128)} %copy-done.5) | copy-start | bytes 1540 | tf_op jit(solution)/shard_map/while
  124.3 3.3 %copy-start.2 = (bf16[2,1152,128]{1,2,0:T(8,128)(2,1)S(1)}, bf16[2,1152,128]{1,2,0:T(8,128)(2,1)}, u32[]{:S(2)}) copy-start(bf16[2,1152,128]{1,2,0:T(8,128)(2,1)} %get-tuple-element.304) | copy-start | bytes 1769476 | tf_op jit(solution)/shard_map/while
  126.5 2.8 %copy-start.6 = (f32[128,1]{0,1:T(1,128)S(1)}, f32[128,1]{0,1:T(1,128)}, u32[]{:S(2)}) copy-start(f32[128,1]{0,1:T(1,128)} %copy-done.5) | copy-start | bytes 1540 | tf_op jit(solution)/shard_map/while
  138.0 3.3 %copy-start.2 = (bf16[2,1152,128]{1,2,0:T(8,128)(2,1)S(1)}, bf16[2,1152,128]{1,2,0:T(8,128)(2,1)}, u32[]{:S(2)}) copy-start(bf16[2,1152,128]{1,2,0:T(8,128)(2,1)} %get-tuple-element.304) | copy-start | bytes 1769476 | tf_op jit(solution)/shard_map/while
  140.2 2.8 %copy-start.6 = (f32[128,1]{0,1:T(1,128)S(1)}, f32[128,1]{0,1:T(1,128)}, u32[]{:S(2)}) copy-start(f32[128,1]{0,1:T(1,128)} %copy-done.5) | copy-start | bytes 1540 | tf_op jit(solution)/shard_map/while
  151.6 3.3 %copy-start.2 = (bf16[2,1152,128]{1,2,0:T(8,128)(2,1)S(1)}, bf16[2,1152,128]{1,2,0:T(8,128)(2,1)}, u32[]{:S(2)}) copy-start(bf16[2,1152,128]{1,2,0:T(8,128)(2,1)} %get-tuple-element.304) | copy-start | bytes 1769476 | tf_op jit(solution)/shard_map/while
  165.3 3.3 %copy-start.2 = (bf16[2,1152,128]{1,2,0:T(8,128)(2,1)S(1)}, bf16[2,1152,128]{1,2,0:T(8,128)(2,1)}, u32[]{:S(2)}) copy-start(bf16[2,1152,128]{1,2,0:T(8,128)(2,1)} %get-tuple-element.304) | copy-start | bytes 1769476 | tf_op jit(solution)/shard_map/while
  167.6 2.8 %copy-start.6 = (f32[128,1]{0,1:T(1,128)S(1)}, f32[128,1]{0,1:T(1,128)}, u32[]{:S(2)}) copy-start(f32[128,1]{0,1:T(1,128)} %copy-done.5) | copy-start | bytes 1540 | tf_op jit(solution)/shard_map/while
  (19 other events, 21.7 us)
where the time goes:
time: 208 us; the launch traced here: 206 us
  other arithmetic  62.6 us (30%)
  blocking collectives  43.4 us (21%)
  starting transfers between devices  37.1 us (18%)
  local copies, waits for them, and re-layouts  29.7 us (14%)
  matrix products  26.4 us (13%)
  waiting for transfers between devices  6.2 us (3%)
    ppermute x8, starting transfers between devices, passed_along(): lax.ppermute(value, axis, [(source, source + steps) for source in range(f...  37.1 us
    all_to_all x1, blocking collectives, on_device(): return lax.all_to_all(mixed, 'cand', 0, 2, tiled=True)  31.8 us
    another operation x26, other arithmetic  28.7 us
    dot_general x8, matrix products, attend_group(): jnp.einsum('rgd,wd->rgw', q_part, key_rot, preferred_element_type=jnp.flo...  18.1 us
    all_gather x1, blocking collectives, on_device(): every_factor = lax.all_gather(factors, 'cand', axis=0, tiled=True)  11.5 us
    while x80, local copies, waits for them, and re-layouts  10.9 us
    dot_general x8, matrix products, attend_group(): jnp.einsum('rgw,wd->rgd', weights, value_rows, preferred_element_type=jnp...  8.29 us
    reduce_sum x8, other arithmetic, attend_group(): total = jnp.sum(expw, axis=-1, keepdims=True)  8.04 us
  transfers between devices with their start and end apart: 8, of which 2 were waited for; matrix products, arithmetic and copies ran while one was open for 2% of the time, Pallas kernels for 0%

commit v1 on v0

--- a/solution.py
+++ b/solution.py
@@ -67,7 +67,12 @@
     group = lax.axis_index("cand")
     query_index = device * row_count + jnp.arange(row_count, dtype=jnp.int32)
     key_index = (device - SPAN) * row_count + jnp.arange((SPAN + 1) * row_count, dtype=jnp.int32)
-    every_factor = lax.all_gather(factors, "cand", axis=0, tiled=True)
+    ring = [factors]
+    for hop in range(7):
+        ring.append(lax.ppermute(ring[-1], "cand", [(dev, (dev + 1) % 8) for dev in range(8)]))
+    every_factor = jnp.roll(
+        jnp.concatenate(ring[::-1], axis=0), (lax.axis_index("cand") + 1) * ring[0].shape[0], axis=0
+    )
     pieces = []
     for distance in range(SPAN, 0, -1):
         pieces.append(passed_along(keys_values, "doc", distance))

time: 208 us -> 220 us (1.058)
  waiting for transfers between devices: 6.2 us -> 30.6 us
  blocking collectives: 43.4 us -> 31.8 us
  other arithmetic: 62.6 us -> 57.4 us
  local copies, waits for them, and re-layouts: 29.7 us -> 33.2 us
    ppermute x0 -> x7, waiting for transfers between devices: none -> 24.4 us  [on_device(): lax.ppermute(ring[-1], 'cand', [(dev, (dev + 1) % 8) for dev in range(8)])]
    all_gather x1 -> x0, blocking collectives: 11.5 us -> none  [on_device(): every_factor = lax.all_gather(factors, 'cand', axis=0, tiled=True)]
    mul x8, other arithmetic: 5.59 us -> 0.12 us  [rotate(): angles = offsets.astype(jnp.float32)[:, None] * inverse[None, :]]
    while x80 -> x112, local copies, waits for them, and re-layouts: 10.9 us -> 12.9 us
  transfers between devices with their start and end apart: 8 -> 15, of which waited for: 2 -> 9; matrix products, arithmetic and copies ran while one was open for 2% -> 2% of each run, Pallas kernels for 0% -> 0%
where the time goes in v1:
time: 220 us; the launch traced here: 219 us
  other arithmetic  57.4 us (26%)
  starting transfers between devices  38.1 us (17%)
  local copies, waits for them, and re-layouts  33.2 us (15%)
  blocking collectives  31.8 us (14%)
  waiting for transfers between devices  30.6 us (14%)
  matrix products  26.4 us (12%)
    ppermute x8, starting transfers between devices, passed_along(): lax.ppermute(value, axis, [(source, source + steps) for source in range(f...  37.1 us
    all_to_all x1, blocking collectives, on_device(): return lax.all_to_all(mixed, 'cand', 0, 2, tiled=True)  31.8 us
    another operation x26, other arithmetic  29 us
    ppermute x7, waiting for transfers between devices, on_device(): lax.ppermute(ring[-1], 'cand', [(dev, (dev + 1) % 8) for dev in range(8)])  24.4 us
    dot_general x8, matrix products, attend_group(): jnp.einsum('rgd,wd->rgw', q_part, key_rot, preferred_element_type=jnp.flo...  18.1 us
    while x112, local copies, waits for them, and re-layouts  12.9 us
    dot_general x8, matrix products, attend_group(): jnp.einsum('rgw,wd->rgd', weights, value_rows, preferred_element_type=jnp...  8.26 us
    reduce_sum x8, other arithmetic, attend_group(): total = jnp.sum(expw, axis=-1, keepdims=True)  8.04 us
  transfers between devices with their start and end apart: 15, of which 9 were waited for; matrix products, arithmetic and copies ran while one was open for 2% of the time, Pallas kernels for 0%

profile of v1, /device:TPU:32, one launch (start us, length us, event | category | flops | bytes accessed | tf_op | source)
XLA Modules:
  0.0 218.7 jit_solution(16919738389233541315)
XLA Ops:
  1.1 5.2 %collective-permute-start.7 = (bf16[2,128,128]{1,2,0:T(8,128)(2,1)S(1)}, bf16[2,128,128]{1,2,0:T(8,128)(2,1)S(1)}, u32[]{:S(2)}, u32[]{:S(2)}) collective-permute-start(bf16[2,128,128]{1,2,0:T(8,128)(2,1)S(1)} %copy.31), channel_id=1, source_target_pairs={{0,8},{1,9},{2,10},{3,11},{4,12},{5,13},{6,14},{7,15},{8,16},{9,17... | collective-permute-start | bytes 196616 | tf_op jit(solution)/shard_map/ppermute | solution.py:17
  6.3 7.2 %collective-permute-start.8 = (bf16[2,128,128]{1,2,0:T(8,128)(2,1)S(1)}, bf16[2,128,128]{1,2,0:T(8,128)(2,1)S(1)}, u32[]{:S(2)}, u32[]{:S(2)}) collective-permute-start(bf16[2,128,128]{1,2,0:T(8,128)(2,1)S(1)} %copy.31), channel_id=1, source_target_pairs={{0,7},{1,8},{2,9},{3,10},{4,11},{5,12},{6,13},{7,14},{8,15},{9,16}... | collective-permute-start | bytes 196616 | tf_op jit(solution)/shard_map/ppermute | solution.py:17
  13.5 5.4 %collective-permute-start.9 = (bf16[2,128,128]{1,2,0:T(8,128)(2,1)S(1)}, bf16[2,128,128]{1,2,0:T(8,128)(2,1)S(1)}, u32[]{:S(2)}, u32[]{:S(2)}) collective-permute-start(bf16[2,128,128]{1,2,0:T(8,128)(2,1)S(1)} %copy.31), channel_id=1, source_target_pairs={{0,6},{1,7},{2,8},{3,9},{4,10},{5,11},{6,12},{7,13},{8,14},{9,15},... | collective-permute-start | bytes 196616 | tf_op jit(solution)/shard_map/ppermute | solution.py:17
  19.0 4.1 %collective-permute-start.10 = (bf16[2,128,128]{1,2,0:T(8,128)(2,1)S(1)}, bf16[2,128,128]{1,2,0:T(8,128)(2,1)S(1)}, u32[]{:S(2)}, u32[]{:S(2)}) collective-permute-start(bf16[2,128,128]{1,2,0:T(8,128)(2,1)S(1)} %copy.31), channel_id=1, source_target_pairs={{0,5},{1,6},{2,7},{3,8},{4,9},{5,10},{6,11},{7,12},{8,13},{9,14},{... | collective-permute-start | bytes 196616 | tf_op jit(solution)/shard_map/ppermute | solution.py:17
  28.5 3.1 %collective-permute-done.1 = f32[1,64]{1,0:T(1,128)S(1)} collective-permute-done((f32[1,64]{1,0:T(1,128)S(1)}, f32[1,64]{1,0:T(1,128)S(1)}, u32[]{:S(2)}, u32[]{:S(2)}) %collective-permute-start.1) | collective-permute-done | bytes 288 | tf_op jit(solution)/shard_map/ppermute | solution.py:72
  31.6 4.1 %collective-permute-done.2 = f32[1,64]{1,0:T(1,128)S(1)} collective-permute-done((f32[1,64]{1,0:T(1,128)S(1)}, f32[1,64]{1,0:T(1,128)S(1)}, u32[]{:S(2)}, u32[]{:S(2)}) %collective-permute-start.2) | collective-permute-done | bytes 288 | tf_op jit(solution)/shard_map/ppermute | solution.py:72
  35.8 4.2 %collective-permute-done.3 = f32[1,64]{1,0:T(1,128)S(1)} collective-permute-done((f32[1,64]{1,0:T(1,128)S(1)}, f32[1,64]{1,0:T(1,128)S(1)}, u32[]{:S(2)}, u32[]{:S(2)}) %collective-permute-start.3) | collective-permute-done | bytes 288 | tf_op jit(solution)/shard_map/ppermute | solution.py:72
  40.0 4.2 %collective-permute-done.4 = f32[1,64]{1,0:T(1,128)S(1)} collective-permute-done((f32[1,64]{1,0:T(1,128)S(1)}, f32[1,64]{1,0:T(1,128)S(1)}, u32[]{:S(2)}, u32[]{:S(2)}) %collective-permute-start.4) | collective-permute-done | bytes 288 | tf_op jit(solution)/shard_map/ppermute | solution.py:72
  44.1 4.2 %collective-permute-done.5 = f32[1,64]{1,0:T(1,128)S(1)} collective-permute-done((f32[1,64]{1,0:T(1,128)S(1)}, f32[1,64]{1,0:T(1,128)S(1)}, u32[]{:S(2)}, u32[]{:S(2)}) %collective-permute-start.5) | collective-permute-done | bytes 288 | tf_op jit(solution)/shard_map/ppermute | solution.py:72
  48.5 4.0 %collective-permute-done.6 = f32[1,64]{1,0:T(1,128)S(1)} collective-permute-done((f32[1,64]{1,0:T(1,128)S(1)}, f32[1,64]{1,0:T(1,128)S(1)}, u32[]{:S(2)}, u32[]{:S(2)}) %collective-permute-start.6) | collective-permute-done | bytes 288 | tf_op jit(solution)/shard_map/ppermute | solution.py:72
  52.5 5.0 %collective-permute-start.11 = (bf16[2,128,128]{1,2,0:T(8,128)(2,1)S(1)}, bf16[2,128,128]{1,2,0:T(8,128)(2,1)S(1)}, u32[]{:S(2)}, u32[]{:S(2)}) collective-permute-start(bf16[2,128,128]{1,2,0:T(8,128)(2,1)S(1)} %copy.31), channel_id=1, source_target_pairs={{0,4},{1,5},{2,6},{3,7},{4,8},{5,9},{6,10},{7,11},{8,12},{9,13},{1... | collective-permute-start | bytes 196616 | tf_op jit(solution)/shard_map/ppermute | solution.py:17
  58.9 4.7 %collective-permute-start.12 = (bf16[2,128,128]{1,2,0:T(8,128)(2,1)S(1)}, bf16[2,128,128]{1,2,0:T(8,128)(2,1)S(1)}, u32[]{:S(2)}, u32[]{:S(2)}) collective-permute-start(bf16[2,128,128]{1,2,0:T(8,128)(2,1)S(1)} %copy.31), channel_id=1, source_target_pairs={{0,3},{1,4},{2,5},{3,6},{4,7},{5,8},{6,9},{7,10},{8,11},{9,12},{10... | collective-permute-start | bytes 196616 | tf_op jit(solution)/shard_map/ppermute | solution.py:17
  63.7 3.4 %collective-permute-start.13 = (bf16[2,128,128]{1,2,0:T(8,128)(2,1)S(1)}, bf16[2,128,128]{1,2,0:T(8,128)(2,1)S(1)}, u32[]{:S(2)}, u32[]{:S(2)}) collective-permute-start(bf16[2,128,128]{1,2,0:T(8,128)(2,1)S(1)} %copy.31), channel_id=1, source_target_pairs={{0,2},{1,3},{2,4},{3,5},{4,6},{5,7},{6,8},{7,9},{8,10},{9,11},{10,... | collective-permute-start | bytes 196616 | tf_op jit(solution)/shard_map/ppermute | solution.py:17
  69.2 3.0 %collective-permute-done.13 = bf16[2,128,128]{1,2,0:T(8,128)(2,1)S(1)} collective-permute-done((bf16[2,128,128]{1,2,0:T(8,128)(2,1)S(1)}, bf16[2,128,128]{1,2,0:T(8,128)(2,1)S(1)}, u32[]{:S(2)}, u32[]{:S(2)}) %collective-permute-start.13) | collective-permute-done | bytes 65568 | tf_op jit(solution)/shard_map/ppermute | solution.py:17
  72.3 3.2 %collective-permute-done.14 = bf16[2,128,128]{1,2,0:T(8,128)(2,1)S(1)} collective-permute-done((bf16[2,128,128]{1,2,0:T(8,128)(2,1)S(1)}, bf16[2,128,128]{1,2,0:T(8,128)(2,1)S(1)}, u32[]{:S(2)}, u32[]{:S(2)}) %collective-permute-start.14) | collective-permute-done | bytes 65568 | tf_op jit(solution)/shard_map/ppermute | solution.py:17
  76.3 106.5 %while.13 = (s32[]{:T(128)}, bf16[8,128,1024]{1,2,0:T(8,128)(2,1)}, bf16[128,1024]{0,1:T(8,128)(2,1)S(1)}, f32[128,1]{0,1:T(1,128)S(1)}, f32[8,64]{1,0:T(8,128)S...) while((s32[]{:T(128)}, bf16[8,128,1024]{1,2,0:T(8,128)(2,1)}, ...), condition=%wide.region_8.9_spmd.clone, body=%wide.region_5.8_spmd.clone.sunk | while | flops 615544960 | bytes 23302068 | solution.py:95
  84.5 2.3 %fusion.49 = (f32[128,8]{0,1:T(8,128)S(1)}, f32[128,8,1152]{2,0,1:T(8,128)S(1)}) fusion(bf16[1152,1,64]{0,2,1:T(8,128)(2,1)S(1)} %get-tuple-element.261, bf16[1152,1,64]{0,2,1:T(8,128)(2,1)S(1)} %get-tuple-element.262, bf16[128,8,64]{2,0,1:T(8,128)(2,1)} %get-tuple-element.267, bf16[128,8,64]{2,0,1:T(8,128)(2,1)} %get-tuple-element.268, ...), kind=kOutput, calls=%fused_computation.67.clone.1 | convolution fusion | flops 306641920 | bytes 5427200 | tf_op jit(solution)/shard_map/while/body/eval_jaxpr/rgd,wd->rgw/dot_general | solution.py:53
  97.8 2.3 %fusion.49 = (f32[128,8]{0,1:T(8,128)S(1)}, f32[128,8,1152]{2,0,1:T(8,128)S(1)}) fusion(bf16[1152,1,64]{0,2,1:T(8,128)(2,1)S(1)} %get-tuple-element.261, bf16[1152,1,64]{0,2,1:T(8,128)(2,1)S(1)} %get-tuple-element.262, bf16[128,8,64]{2,0,1:T(8,128)(2,1)} %get-tuple-element.267, bf16[128,8,64]{2,0,1:T(8,128)(2,1)} %get-tuple-element.268, ...), kind=kOutput, calls=%fused_computation.67.clone.1 | convolution fusion | flops 306641920 | bytes 5427200 | tf_op jit(solution)/shard_map/while/body/eval_jaxpr/rgd,wd->rgw/dot_general | solution.py:53
  111.2 2.3 %fusion.49 = (f32[128,8]{0,1:T(8,128)S(1)}, f32[128,8,1152]{2,0,1:T(8,128)S(1)}) fusion(bf16[1152,1,64]{0,2,1:T(8,128)(2,1)S(1)} %get-tuple-element.261, bf16[1152,1,64]{0,2,1:T(8,128)(2,1)S(1)} %get-tuple-element.262, bf16[128,8,64]{2,0,1:T(8,128)(2,1)} %get-tuple-element.267, bf16[128,8,64]{2,0,1:T(8,128)(2,1)} %get-tuple-element.268, ...), kind=kOutput, calls=%fused_computation.67.clone.1 | convolution fusion | flops 306641920 | bytes 5427200 | tf_op jit(solution)/shard_map/while/body/eval_jaxpr/rgd,wd->rgw/dot_general | solution.py:53
  124.5 2.3 %fusion.49 = (f32[128,8]{0,1:T(8,128)S(1)}, f32[128,8,1152]{2,0,1:T(8,128)S(1)}) fusion(bf16[1152,1,64]{0,2,1:T(8,128)(2,1)S(1)} %get-tuple-element.261, bf16[1152,1,64]{0,2,1:T(8,128)(2,1)S(1)} %get-tuple-element.262, bf16[128,8,64]{2,0,1:T(8,128)(2,1)} %get-tuple-element.267, bf16[128,8,64]{2,0,1:T(8,128)(2,1)} %get-tuple-element.268, ...), kind=kOutput, calls=%fused_computation.67.clone.1 | convolution fusion | flops 306641920 | bytes 5427200 | tf_op jit(solution)/shard_map/while/body/eval_jaxpr/rgd,wd->rgw/dot_general | solution.py:53
  137.8 2.3 %fusion.49 = (f32[128,8]{0,1:T(8,128)S(1)}, f32[128,8,1152]{2,0,1:T(8,128)S(1)}) fusion(bf16[1152,1,64]{0,2,1:T(8,128)(2,1)S(1)} %get-tuple-element.261, bf16[1152,1,64]{0,2,1:T(8,128)(2,1)S(1)} %get-tuple-element.262, bf16[128,8,64]{2,0,1:T(8,128)(2,1)} %get-tuple-element.267, bf16[128,8,64]{2,0,1:T(8,128)(2,1)} %get-tuple-element.268, ...), kind=kOutput, calls=%fused_computation.67.clone.1 | convolution fusion | flops 306641920 | bytes 5427200 | tf_op jit(solution)/shard_map/while/body/eval_jaxpr/rgd,wd->rgw/dot_general | solution.py:53
  151.1 2.3 %fusion.49 = (f32[128,8]{0,1:T(8,128)S(1)}, f32[128,8,1152]{2,0,1:T(8,128)S(1)}) fusion(bf16[1152,1,64]{0,2,1:T(8,128)(2,1)S(1)} %get-tuple-element.261, bf16[1152,1,64]{0,2,1:T(8,128)(2,1)S(1)} %get-tuple-element.262, bf16[128,8,64]{2,0,1:T(8,128)(2,1)} %get-tuple-element.267, bf16[128,8,64]{2,0,1:T(8,128)(2,1)} %get-tuple-element.268, ...), kind=kOutput, calls=%fused_computation.67.clone.1 | convolution fusion | flops 306641920 | bytes 5427200 | tf_op jit(solution)/shard_map/while/body/eval_jaxpr/rgd,wd->rgw/dot_general | solution.py:53
  182.8 31.8 %all_to_all.18 = bf16[8,128,1024]{1,2,0:T(8,128)(2,1)} all-to-all(bf16[8,128,1024]{1,2,0:T(8,128)(2,1)} %get-tuple-element.110), channel_id=1, replica_groups=mesh['cand'=8,'doc'=64] {'cand'}, dimensions={0} | all-to-all | bytes 4194304 | tf_op jit(solution)/shard_map/all_to_all | solution.py:96
  214.6 4.1 %copy.42 = bf16[1,128,8192]{2,1,0:T(8,128)(2,1)} copy(bf16[1,128,8192]{1,2,0:T(8,128)(2,1)} %bitcast.45) | data formatting | bytes 4194304 | tf_op jit(solution)/shard_map/all_to_all | solution.py:96
  (252 shorter events, 103.0 us)
Async XLA Ops:
  0.0 31.6 %copy-start = (bf16[128,8192]{1,0:T(8,128)(2,1)S(1)}, bf16[128,8192]{1,0:T(8,128)(2,1)}, u32[]{:S(2)}) copy-start(bf16[128,8192]{1,0:T(8,128)(2,1)} %param.6) | copy-start | bytes 6291460
  1.1 57.8 %collective-permute-start.7 = (bf16[2,128,128]{1,2,0:T(8,128)(2,1)S(1)}, bf16[2,128,128]{1,2,0:T(8,128)(2,1)S(1)}, u32[]{:S(2)}, u32[]{:S(2)}) collective-permute-start(bf16[2,128,128]{1,2,0:T(8,128)(2,1)S(1)} %copy.31), channel_id=1, source_target_pairs={{0,8},{1,9},{2,10},{3,11},{4,12},{5,13},{6,14},{7,15},{8,16},{9,17... | collective-permute-start | bytes 196616 | tf_op jit(solution)/shard_map/ppermute | solution.py:17
  6.3 57.4 %collective-permute-start.8 = (bf16[2,128,128]{1,2,0:T(8,128)(2,1)S(1)}, bf16[2,128,128]{1,2,0:T(8,128)(2,1)S(1)}, u32[]{:S(2)}, u32[]{:S(2)}) collective-permute-start(bf16[2,128,128]{1,2,0:T(8,128)(2,1)S(1)} %copy.31), channel_id=1, source_target_pairs={{0,7},{1,8},{2,9},{3,10},{4,11},{5,12},{6,13},{7,14},{8,15},{9,16}... | collective-permute-start | bytes 196616 | tf_op jit(solution)/shard_map/ppermute | solution.py:17
  13.5 53.6 %collective-permute-start.9 = (bf16[2,128,128]{1,2,0:T(8,128)(2,1)S(1)}, bf16[2,128,128]{1,2,0:T(8,128)(2,1)S(1)}, u32[]{:S(2)}, u32[]{:S(2)}) collective-permute-start(bf16[2,128,128]{1,2,0:T(8,128)(2,1)S(1)} %copy.31), channel_id=1, source_target_pairs={{0,6},{1,7},{2,8},{3,9},{4,10},{5,11},{6,12},{7,13},{8,14},{9,15},... | collective-permute-start | bytes 196616 | tf_op jit(solution)/shard_map/ppermute | solution.py:17
  19.0 50.1 %collective-permute-start.10 = (bf16[2,128,128]{1,2,0:T(8,128)(2,1)S(1)}, bf16[2,128,128]{1,2,0:T(8,128)(2,1)S(1)}, u32[]{:S(2)}, u32[]{:S(2)}) collective-permute-start(bf16[2,128,128]{1,2,0:T(8,128)(2,1)S(1)} %copy.31), channel_id=1, source_target_pairs={{0,5},{1,6},{2,7},{3,8},{4,9},{5,10},{6,11},{7,12},{8,13},{9,14},{... | collective-permute-start | bytes 196616 | tf_op jit(solution)/shard_map/ppermute | solution.py:17
  23.1 4.3 %collective-permute-start = (f32[1,64]{1,0:T(1,128)}, f32[1,64]{1,0:T(1,128)S(1)}, u32[]{:S(2)}, u32[]{:S(2)}) collective-permute-start(f32[1,64]{1,0:T(1,128)} %param.8), channel_id=1, source_target_pairs={{0,64},{64,128},{128,192},{192,256},{256,320},{320,384},{384,448},... | collective-permute-start | bytes 776 | tf_op jit(solution)/shard_map/ppermute | solution.py:72
  25.5 27.0 %copy-start.4 = (s32[128]{0:T(128)}, s32[128]{0:T(128)S(1)}, u32[]{:S(2)}) copy-start(s32[128]{0:T(128)S(1)} %iota_add_fusion.1) | copy-start | bytes 1540
  27.4 4.2 %collective-permute-start.1 = (f32[1,64]{1,0:T(1,128)S(1)}, f32[1,64]{1,0:T(1,128)S(1)}, u32[]{:S(2)}, u32[]{:S(2)}) collective-permute-start(f32[1,64]{1,0:T(1,128)S(1)} %collective-permute-done), channel_id=1, source_target_pairs={{0,64},{64,128},{128,192},{192,256},{256,320},{320,384},{384,448},... | collective-permute-start | bytes 776 | tf_op jit(solution)/shard_map/ppermute | solution.py:72
  31.6 4.2 %collective-permute-start.2 = (f32[1,64]{1,0:T(1,128)S(1)}, f32[1,64]{1,0:T(1,128)S(1)}, u32[]{:S(2)}, u32[]{:S(2)}) collective-permute-start(f32[1,64]{1,0:T(1,128)S(1)} %collective-permute-done.1), channel_id=1, source_target_pairs={{0,64},{64,128},{128,192},{192,256},{256,320},{320,384},{384,448},... | collective-permute-start | bytes 776 | tf_op jit(solution)/shard_map/ppermute | solution.py:72
  35.8 4.2 %collective-permute-start.3 = (f32[1,64]{1,0:T(1,128)S(1)}, f32[1,64]{1,0:T(1,128)S(1)}, u32[]{:S(2)}, u32[]{:S(2)}) collective-permute-start(f32[1,64]{1,0:T(1,128)S(1)} %collective-permute-done.2), channel_id=1, source_target_pairs={{0,64},{64,128},{128,192},{192,256},{256,320},{320,384},{384,448},... | collective-permute-start | bytes 776 | tf_op jit(solution)/shard_map/ppermute | solution.py:72
  40.0 4.2 %collective-permute-start.4 = (f32[1,64]{1,0:T(1,128)S(1)}, f32[1,64]{1,0:T(1,128)S(1)}, u32[]{:S(2)}, u32[]{:S(2)}) collective-permute-start(f32[1,64]{1,0:T(1,128)S(1)} %collective-permute-done.3), channel_id=1, source_target_pairs={{0,64},{64,128},{128,192},{192,256},{256,320},{320,384},{384,448},... | collective-permute-start | bytes 776 | tf_op jit(solution)/shard_map/ppermute | solution.py:72
  44.1 4.2 %collective-permute-start.5 = (f32[1,64]{1,0:T(1,128)S(1)}, f32[1,64]{1,0:T(1,128)S(1)}, u32[]{:S(2)}, u32[]{:S(2)}) collective-permute-start(f32[1,64]{1,0:T(1,128)S(1)} %collective-permute-done.4), channel_id=1, source_target_pairs={{0,64},{64,128},{128,192},{192,256},{256,320},{320,384},{384,448},... | collective-permute-start | bytes 776 | tf_op jit(solution)/shard_map/ppermute | solution.py:72
  48.3 4.2 %collective-permute-start.6 = (f32[1,64]{1,0:T(1,128)S(1)}, f32[1,64]{1,0:T(1,128)S(1)}, u32[]{:S(2)}, u32[]{:S(2)}) collective-permute-start(f32[1,64]{1,0:T(1,128)S(1)} %collective-permute-done.5), channel_id=1, source_target_pairs={{0,64},{64,128},{128,192},{192,256},{256,320},{320,384},{384,448},... | collective-permute-start | bytes 776 | tf_op jit(solution)/shard_map/ppermute | solution.py:72
  52.5 16.6 %collective-permute-start.11 = (bf16[2,128,128]{1,2,0:T(8,128)(2,1)S(1)}, bf16[2,128,128]{1,2,0:T(8,128)(2,1)S(1)}, u32[]{:S(2)}, u32[]{:S(2)}) collective-permute-start(bf16[2,128,128]{1,2,0:T(8,128)(2,1)S(1)} %copy.31), channel_id=1, source_target_pairs={{0,4},{1,5},{2,6},{3,7},{4,8},{5,9},{6,10},{7,11},{8,12},{9,13},{1... | collective-permute-start | bytes 196616 | tf_op jit(solution)/shard_map/ppermute | solution.py:17
  58.9 10.3 %collective-permute-start.12 = (bf16[2,128,128]{1,2,0:T(8,128)(2,1)S(1)}, bf16[2,128,128]{1,2,0:T(8,128)(2,1)S(1)}, u32[]{:S(2)}, u32[]{:S(2)}) collective-permute-start(bf16[2,128,128]{1,2,0:T(8,128)(2,1)S(1)} %copy.31), channel_id=1, source_target_pairs={{0,3},{1,4},{2,5},{3,6},{4,7},{5,8},{6,9},{7,10},{8,11},{9,12},{10... | collective-permute-start | bytes 196616 | tf_op jit(solution)/shard_map/ppermute | solution.py:17
  63.7 8.6 %collective-permute-start.13 = (bf16[2,128,128]{1,2,0:T(8,128)(2,1)S(1)}, bf16[2,128,128]{1,2,0:T(8,128)(2,1)S(1)}, u32[]{:S(2)}, u32[]{:S(2)}) collective-permute-start(bf16[2,128,128]{1,2,0:T(8,128)(2,1)S(1)} %copy.31), channel_id=1, source_target_pairs={{0,2},{1,3},{2,4},{3,5},{4,6},{5,7},{6,8},{7,9},{8,10},{9,11},{10,... | collective-permute-start | bytes 196616 | tf_op jit(solution)/shard_map/ppermute | solution.py:17
  67.1 8.3 %collective-permute-start.14 = (bf16[2,128,128]{1,2,0:T(8,128)(2,1)S(1)}, bf16[2,128,128]{1,2,0:T(8,128)(2,1)S(1)}, u32[]{:S(2)}, u32[]{:S(2)}) collective-permute-start(bf16[2,128,128]{1,2,0:T(8,128)(2,1)S(1)} %copy.31), channel_id=1, source_target_pairs={{0,1},{1,2},{2,3},{3,4},{4,5},{5,6},{6,7},{7,8},{8,9},{9,10},{10,1... | collective-permute-start | bytes 196616 | tf_op jit(solution)/shard_map/ppermute | solution.py:17
  84.5 3.3 %copy-start.2 = (bf16[2,1152,128]{1,2,0:T(8,128)(2,1)S(1)}, bf16[2,1152,128]{1,2,0:T(8,128)(2,1)}, u32[]{:S(2)}) copy-start(bf16[2,1152,128]{1,2,0:T(8,128)(2,1)} %get-tuple-element.304) | copy-start | bytes 1769476 | tf_op jit(solution)/shard_map/while
  97.8 3.3 %copy-start.2 = (bf16[2,1152,128]{1,2,0:T(8,128)(2,1)S(1)}, bf16[2,1152,128]{1,2,0:T(8,128)(2,1)}, u32[]{:S(2)}) copy-start(bf16[2,1152,128]{1,2,0:T(8,128)(2,1)} %get-tuple-element.304) | copy-start | bytes 1769476 | tf_op jit(solution)/shard_map/while
  111.2 3.3 %copy-start.2 = (bf16[2,1152,128]{1,2,0:T(8,128)(2,1)S(1)}, bf16[2,1152,128]{1,2,0:T(8,128)(2,1)}, u32[]{:S(2)}) copy-start(bf16[2,1152,128]{1,2,0:T(8,128)(2,1)} %get-tuple-element.304) | copy-start | bytes 1769476 | tf_op jit(solution)/shard_map/while
  124.5 3.3 %copy-start.2 = (bf16[2,1152,128]{1,2,0:T(8,128)(2,1)S(1)}, bf16[2,1152,128]{1,2,0:T(8,128)(2,1)}, u32[]{:S(2)}) copy-start(bf16[2,1152,128]{1,2,0:T(8,128)(2,1)} %get-tuple-element.304) | copy-start | bytes 1769476 | tf_op jit(solution)/shard_map/while
  137.8 3.3 %copy-start.2 = (bf16[2,1152,128]{1,2,0:T(8,128)(2,1)S(1)}, bf16[2,1152,128]{1,2,0:T(8,128)(2,1)}, u32[]{:S(2)}) copy-start(bf16[2,1152,128]{1,2,0:T(8,128)(2,1)} %get-tuple-element.304) | copy-start | bytes 1769476 | tf_op jit(solution)/shard_map/while
  151.1 3.3 %copy-start.2 = (bf16[2,1152,128]{1,2,0:T(8,128)(2,1)S(1)}, bf16[2,1152,128]{1,2,0:T(8,128)(2,1)}, u32[]{:S(2)}) copy-start(bf16[2,1152,128]{1,2,0:T(8,128)(2,1)} %get-tuple-element.304) | copy-start | bytes 1769476 | tf_op jit(solution)/shard_map/while
  164.4 3.3 %copy-start.2 = (bf16[2,1152,128]{1,2,0:T(8,128)(2,1)S(1)}, bf16[2,1152,128]{1,2,0:T(8,128)(2,1)}, u32[]{:S(2)}) copy-start(bf16[2,1152,128]{1,2,0:T(8,128)(2,1)} %get-tuple-element.304) | copy-start | bytes 1769476 | tf_op jit(solution)/shard_map/while
  (42 other events, 68.3 us)
